TPU v7x, 512 devices: a whole 4x4x16 slice. The times are simulated.
512 devices in a mesh: mem: 16 (over z_hi, y, core), gx: 32 (over x, z_lo).
Axes of the slice: x: 4, y: 4, z: 16 (z_hi: 2, z_lo: 8; z = z_hi * 8 + z_lo), core: 2. Of those that a mesh axis runs over, the one named last changes fastest.
Arguments:
- weights: bfloat16 [16, 512, 32768], P('mem', 'gx'), may hold values from -6 to 6
- perturbations: bfloat16 [2, 16, 512, 32768], P(None, 'mem', 'gx'), may hold values from -3 to 3
- obs_cell: int32 [131072], P('gx'), may hold values from 0 to 524287
- obs_slot: int32 [131072], P('gx'), may hold values from 0 to 1
- innovation: float32 [131072], P('gx'), may hold values from -24 to 24
- obs_weight: float32 [131072], P('gx'), may hold values from 0.5 to 4
- obs_count: int32 [32], P('gx'), may hold values from 2048 to 4096, as said below
Outputs:
- gradient: float32 [16, 512, 32768], P('mem', 'gx')
Inputs may be any that keep to these rules, and one draw needn't show every extreme that they name: Slab s uses its first obs_count[s] observation slots, o = s * 4096 .. s * 4096 + obs_count[s] - 1; some slab is full and another holds 2048. `obs_cell`: the cell is numbered (x within the slab) * 512 * 64 + y * 64 + z; several observations may share a cell.
All inputs are finite; a program needn't handle non-finite values.
Results may differ from a plain program's by a relative error of at most 0.0029.
Values may be sent and summed in bfloat16 or wider, within the bound.
No kernel may reach another device: no remote copies, remote signals or barrier semaphores. Data moves between devices by JAX's collectives and lax.ppermute only.
A program may use at most 64 MiB of HBM per device.

v0:
```python
import numpy as np
import jax
import jax.numpy as jnp
from jax import lax
from jax.sharding import PartitionSpec as P

NY = 512
NZ = 64
LANES = 128
tap_reach = 15
corr_scale = 7.0


def padded_2(block, sides, width):
    for axis, dim in sides:
        count = lax.axis_size(axis)
        forward = [(i, i + 1) for i in range(count - 1)]
        backward = [(target, source) for source, target in forward]
        low = lax.ppermute(
            lax.slice_in_dim(block, block.shape[dim] - width, None, axis=dim), axis, forward
        )
        high = lax.ppermute(lax.slice_in_dim(block, 0, width, axis=dim), axis, backward)
        block = jnp.concatenate([low, block, high], axis=dim)
    return block


def tap_values():
    offsets = np.arange(-tap_reach, tap_reach + 1).astype(np.float32)
    bell = np.exp(-offsets * offsets / np.float32(2.0 * corr_scale * corr_scale)).astype(np.float32)
    taps = (bell / np.sqrt(np.sum(bell * bell, dtype=np.float32))).astype(np.float32)
    return taps.astype(jnp.bfloat16).astype(np.float32)


def band_matrix(count_out, count_in, start):
    out_pos = np.arange(count_out)
    in_pos = np.arange(count_in)
    offsets = in_pos[None, :] - out_pos[:, None] - start
    taps = tap_values()
    lookup = taps[np.clip(offsets + tap_reach, 0, 2 * tap_reach)]
    band = np.where(np.abs(offsets) <= tap_reach, lookup, np.zeros_like(lookup))
    return jnp.asarray(band.astype(jnp.bfloat16))


def along_z(field):
    members, slab_rows, plane_cells = field.shape
    band_z = band_matrix(NZ, NZ, 0)
    grid = field.reshape(members, slab_rows, NY, NZ)
    result = jnp.einsum("mxyq,zq->mxyz", grid, band_z, preferred_element_type=jnp.float32)
    return result.reshape(members, slab_rows, plane_cells)


def along_y(field):
    members, slab_rows, plane_cells = field.shape
    band_y = band_matrix(NY, NY, 0)
    grid = field.reshape(members, slab_rows, NY, NZ)
    result = jnp.einsum("mxqz,yq->mxyz", grid, band_y, preferred_element_type=jnp.float32)
    return result.reshape(members, slab_rows, plane_cells)


def along_x(padded, slab_rows):
    band_x = band_matrix(slab_rows, slab_rows + 2 * tap_reach, tap_reach)
    return jnp.einsum("ip,mpc->mic", band_x, padded, preferred_element_type=jnp.float32)


def local(weights, perturbations, obs_cell, obs_slot, innovation, obs_weight, obs_count):
    members, slab_rows, plane_cells = weights.shape
    slot_count = perturbations.shape[0]
    nobs = obs_cell.shape[0]
    rows = slab_rows * plane_cells // LANES
    z_smooth = along_z(weights).astype(jnp.bfloat16)
    y_smooth = along_y(z_smooth).astype(jnp.bfloat16)
    padded = padded_2(y_smooth, (("gx", 1),), tap_reach)
    smoothed = along_x(padded, slab_rows)
    obs_row = obs_cell // LANES
    lane_hit = lax.broadcasted_iota(jnp.int32, (nobs, LANES), 1) == (obs_cell % LANES)[:, None]
    s_rows = smoothed.reshape(rows, LANES)[obs_row]
    s_val = jnp.sum(jnp.where(lane_hit, s_rows, 0.0), axis=1)
    p_rows = perturbations.reshape(slot_count * rows, LANES)[obs_slot * rows + obs_row]
    p_val = jnp.sum(jnp.where(lane_hit, p_rows.astype(jnp.float32), 0.0), axis=1)
    sampled = lax.psum(p_val * s_val, "mem")
    live_mask = (jnp.arange(nobs) < obs_count[0]).astype(jnp.float32)
    residual = live_mask * obs_weight * (sampled - innovation)
    contrib = jnp.where(lane_hit, (p_val * residual)[:, None], 0.0)
    adjoint = jnp.zeros((rows, LANES), jnp.float32).at[obs_row].add(contrib)
    adjoint_source = adjoint.reshape(members, slab_rows, plane_cells).astype(jnp.bfloat16)
    padded_back = padded_2(adjoint_source, (("gx", 1),), tap_reach)
    x_back = along_x(padded_back, slab_rows).astype(jnp.bfloat16)
    y_back = along_y(x_back).astype(jnp.bfloat16)
    return weights.astype(jnp.float32) + along_z(y_back)


def solution(mesh):
    return jax.shard_map(
        local,
        mesh=mesh,
        in_specs=(
            P("mem", "gx", None),
            P(None, "mem", "gx", None),
            P("gx"),
            P("gx"),
            P("gx"),
            P("gx"),
            P("gx"),
        ),
        out_specs=P("mem", "gx", None),
        check_vma=False,
    )
```

profile of v0, /device:TPU:2, one launch (start us, length us, event | category | flops | bytes accessed | tf_op | source)
XLA Modules:
  0.0 301.9 jit_solution(14526492323340186401)
XLA Ops:
  0.0 3.1 %reshape.82 = bf16[16,512,64]{2,1,0:T(8,128)(2,1)S(1)} reshape(bf16[1,16,32768]{2,1,0:T(8,128)(2,1)} %param.13) | data formatting | bytes 2097152 | tf_op jit(solution)/shard_map/reshape
  3.1 2.4 fusion.14
  5.5 2.0 copy.15
  7.6 1.7 convert_element_type.82
  9.3 1.5 fusion.25
  10.8 3.8 %collective-permute-start = (bf16[1,15,32768]{2,1,0:T(8,128)(2,1)}, bf16[1,15,32768]{2,1,0:T(8,128)(2,1)}, u32[]{:S(2)}, u32[]{:S(2)}) collective-permute-start(bf16[1,15,32768]{2,1,0:T(8,128)(2,1)} %get-tuple-element.11), channel_id=1, source_target_pairs={{0,1},{1,2},{2,3},{3,4},{4,5},{5,6},{6,7},{7,8},{8,9},{9,10},{10,1... | collective-permute-start | bytes 2949128 | tf_op jit(solution)/shard_map/ppermute | solution.py:19
  14.6 0.0 copy-start.7
  14.7 0.0 copy-start.8
  14.7 11.2 %collective-permute-start.1 = (bf16[1,15,32768]{2,1,0:T(8,128)(2,1)}, bf16[1,15,32768]{2,1,0:T(8,128)(2,1)}, u32[]{:S(2)}, u32[]{:S(2)}) collective-permute-start(bf16[1,15,32768]{2,1,0:T(8,128)(2,1)} %get-tuple-element.12), channel_id=1, source_target_pairs={{1,0},{2,1},{3,2},{4,3},{5,4},{6,5},{7,6},{8,7},{9,8},{10,9},{11,1... | collective-permute-start | bytes 2949128 | tf_op jit(solution)/shard_map/ppermute | solution.py:22
  25.9 2.9 reshape.81
  29.5 0.0 copy-start.9
  29.5 15.0 %gather_fusion = bf16[4096,128]{1,0:T(8,128)(2,1)} fusion(bf16[8192,128]{1,0:T(8,128)(2,1)S(1)} %reshape.81, s32[4096]{0:T(1024)S(1)} %get-tuple-element.13), kind=kCustom, calls=%fused_computation | custom fusion | bytes 2113536 | tf_op jit(solution)/shard_map/gather | solution.py:78
  44.5 3.8 %collective-permute-done = bf16[1,15,32768]{2,1,0:T(8,128)(2,1)} collective-permute-done((bf16[1,15,32768]{2,1,0:T(8,128)(2,1)}, bf16[1,15,32768]{2,1,0:T(8,128)(2,1)}, u32[]{:S(2)}, u32[]{:S(2)}) %collective-permute-start) | collective-permute-done | bytes 983072 | tf_op jit(solution)/shard_map/ppermute | solution.py:19
  48.3 15.8 %collective-permute-done.1 = bf16[1,15,32768]{2,1,0:T(8,128)(2,1)} collective-permute-done((bf16[1,15,32768]{2,1,0:T(8,128)(2,1)}, bf16[1,15,32768]{2,1,0:T(8,128)(2,1)}, u32[]{:S(2)}, u32[]{:S(2)}) %collective-permute-start.1) | collective-permute-done | bytes 983072 | tf_op jit(solution)/shard_map/ppermute | solution.py:22
  64.2 3.8 %convolution_bitcast_fusion = f32[1,16,32768]{2,1,0:T(8,128)} fusion(bf16[16,46]{1,0:T(8,128)(2,1)S(1)} %copy-done.9, bf16[1,15,32768]{2,1,0:T(8,128)(2,1)} %collective-permute-done.1, bf16[1,16,32768]{2,1,0:T(8,128)(2,1)S(1)} %convert_element_type.82, bf16[1,15,32768]{2,1,0:T(8,128)(2,1)} %collective-permute-done), kind=kOutput, calls=%fused_computation.3 | convolution fusion | flops 57278464 | bytes 5113280 | tf_op jit(solution)/shard_map/ip,mpc->mic/dot_general | solution.py:62
  68.0 1.7 reshape.84
  69.7 14.2 %gather_fusion.1 = f32[4096,128]{1,0:T(8,128)} fusion(f32[4096,128]{1,0:T(8,128)S(1)} %reshape.84, s32[4096]{0:T(1024)S(1)} %get-tuple-element.7), kind=kCustom, calls=%fused_computation.1 | custom fusion | bytes 4210688 | tf_op jit(solution)/shard_map/gather | solution.py:76
  83.9 2.8 select_reduce_fusion
  86.8 136.0 %psum.7 = f32[4096]{0:T(1024)S(1)} all-reduce(f32[4096]{0:T(1024)S(1)} %mul.17), channel_id=1, replica_groups=mesh['mem'=16,'gx'=32] {'mem'}, use_global_device_ids=true, to_apply=%region_2.3 | all-reduce | flops 4096 | bytes 32768 | tf_op jit(solution)/shard_map/psum | solution.py:80
  222.8 25.4 %scatter_custom_fusion = f32[4096,128]{1,0:T(8,128)S(1)} fusion(s32[4096]{0:T(1024)S(1)} %get-tuple-element.8, f32[4096]{0:T(1024)S(1)} %multiply_multiply_fusion, s32[4096]{0:T(1024)S(1)} %get-tuple-element.14, f32[]{:T(128)} %constant.34.clone.1), kind=kCustom, calls=%fused_computation.20 | custom fusion | flops 1572864 | bytes 2130944 | tf_op jit(solution)/shard_map/scatter-add | solution.py:84
  248.2 0.1 convert_element_type.83
  248.3 0.5 convert_element_type.84
  248.8 0.2 fusion.24
  249.1 2.9 collective-permute-start.2
  251.9 10.7 %collective-permute-start.3 = (bf16[1,15,32768]{2,1,0:T(8,128)(2,1)S(1)}, bf16[1,15,32768]{2,1,0:T(8,128)(2,1)S(1)}, u32[]{:S(2)}, u32[]{:S(2)}) collective-permute-start(bf16[1,15,32768]{2,1,0:T(8,128)(2,1)S(1)} %get-tuple-element.10), channel_id=1, source_target_pairs={{1,0},{2,1},{3,2},{4,3},{5,4},{6,5},{7,6},{8,7},{9,8},{10,9},{11,1... | collective-permute-start | bytes 2949128 | tf_op jit(solution)/shard_map/ppermute | solution.py:22
  262.6 19.7 %collective-permute-done.2 = bf16[1,15,32768]{2,1,0:T(8,128)(2,1)S(1)} collective-permute-done((bf16[1,15,32768]{2,1,0:T(8,128)(2,1)S(1)}, bf16[1,15,32768]{2,1,0:T(8,128)(2,1)S(1)}, u32[]{:S(2)}, u32[]{:S(2)}) %collective-permute-start.2) | collective-permute-done | bytes 983072 | tf_op jit(solution)/shard_map/ppermute | solution.py:19
  282.3 6.2 %collective-permute-done.3 = bf16[1,15,32768]{2,1,0:T(8,128)(2,1)S(1)} collective-permute-done((bf16[1,15,32768]{2,1,0:T(8,128)(2,1)S(1)}, bf16[1,15,32768]{2,1,0:T(8,128)(2,1)S(1)}, u32[]{:S(2)}, u32[]{:S(2)}) %collective-permute-start.3) | collective-permute-done | bytes 983072 | tf_op jit(solution)/shard_map/ppermute | solution.py:22
  288.4 2.0 fusion
  290.4 3.1 %reshape.86 = bf16[16,512,64]{2,1,0:T(8,128)(2,1)S(1)} reshape(bf16[1,16,32768]{2,1,0:T(8,128)(2,1)} %fusion) | data formatting | bytes 2097152 | tf_op jit(solution)/shard_map/reshape.9
  293.5 3.8 %fusion.15 = f32[16,512,64]{2,1,0:T(8,128)} fusion(bf16[64,64,1]{1,0,2:T(8,128)(2,1)S(1)} %copy-done.4, bf16[16,512,64]{2,1,0:T(8,128)(2,1)S(1)} %reshape.86, bf16[512,512,1]{1,0,2:T(8,128)(2,1)S(1)} %copy-done.3), kind=kOutput, calls=%fused_computation.28 | convolution fusion | flops 604504064 | bytes 3678208 | tf_op jit(solution)/shard_map/mxyq,zq->mxyz/dot_general | solution.py:48
  297.4 3.0 reshape.88
  300.4 1.5 convert_add_fusion
  (20 shorter events, 0.1 us)
Async XLA Ops:
  0.0 3.1 %copy-start.4 = (bf16[64,64,1]{1,0,2:T(8,128)(2,1)S(1)}, bf16[64,64,1]{1,0,2:T(8,128)(2,1)}, u32[]{:S(2)}) copy-start(bf16[64,64,1]{1,0,2:T(8,128)(2,1)} %constant.49) | copy-start | bytes 24580
  0.0 3.1 %copy-start.2 = (bf16[512,512,1]{1,0,2:T(8,128)(2,1)S(1)}, bf16[512,512,1]{1,0,2:T(8,128)(2,1)}, u32[]{:S(2)}) copy-start(bf16[512,512,1]{1,0,2:T(8,128)(2,1)} %constant.50) | copy-start | bytes 1572868
  10.8 37.5 %collective-permute-start = (bf16[1,15,32768]{2,1,0:T(8,128)(2,1)}, bf16[1,15,32768]{2,1,0:T(8,128)(2,1)}, u32[]{:S(2)}, u32[]{:S(2)}) collective-permute-start(bf16[1,15,32768]{2,1,0:T(8,128)(2,1)} %get-tuple-element.11), channel_id=1, source_target_pairs={{0,1},{1,2},{2,3},{3,4},{4,5},{5,6},{6,7},{7,8},{8,9},{9,10},{10,1... | collective-permute-start | bytes 2949128 | tf_op jit(solution)/shard_map/ppermute | solution.py:19
  14.6 14.8 %copy-start.7 = (s32[4096]{0:T(1024)S(1)}, s32[4096]{0:T(1024)}, u32[]{:S(2)}) copy-start(s32[4096]{0:T(1024)} %param.15) | copy-start | bytes 49156
  14.7 14.8 %copy-start.8 = (s32[4096]{0:T(1024)S(1)}, s32[4096]{0:T(1024)}, u32[]{:S(2)}) copy-start(s32[4096]{0:T(1024)} %param.16) | copy-start | bytes 49156
  14.7 49.5 %collective-permute-start.1 = (bf16[1,15,32768]{2,1,0:T(8,128)(2,1)}, bf16[1,15,32768]{2,1,0:T(8,128)(2,1)}, u32[]{:S(2)}, u32[]{:S(2)}) collective-permute-start(bf16[1,15,32768]{2,1,0:T(8,128)(2,1)} %get-tuple-element.12), channel_id=1, source_target_pairs={{1,0},{2,1},{3,2},{4,3},{5,4},{6,5},{7,6},{8,7},{9,8},{10,9},{11,1... | collective-permute-start | bytes 2949128 | tf_op jit(solution)/shard_map/ppermute | solution.py:22
  29.5 34.7 %copy-start.9 = (bf16[16,46]{1,0:T(8,128)(2,1)S(1)}, bf16[16,46]{1,0:T(8,128)(2,1)}, u32[]{:S(2)}) copy-start(bf16[16,46]{1,0:T(8,128)(2,1)} %constant.45.clone) | copy-start | bytes 4420
  69.7 14.2 %copy-start.1 = (bf16[4096,128]{1,0:T(8,128)(2,1)S(1)}, bf16[4096,128]{1,0:T(8,128)(2,1)}, u32[]{:S(2)}) copy-start(bf16[4096,128]{1,0:T(8,128)(2,1)} %gather_fusion) | copy-start | bytes 3145732
  83.9 138.8 %copy-start.5 = (f32[4096]{0:T(1024)S(1)}, f32[4096]{0:T(1024)}, u32[]{:S(2)}) copy-start(f32[4096]{0:T(1024)} %param.17) | copy-start | bytes 49156
  83.9 138.8 %copy-start.6 = (f32[4096]{0:T(1024)S(1)}, f32[4096]{0:T(1024)}, u32[]{:S(2)}) copy-start(f32[4096]{0:T(1024)} %param.18) | copy-start | bytes 49156
  249.1 33.2 %collective-permute-start.2 = (bf16[1,15,32768]{2,1,0:T(8,128)(2,1)S(1)}, bf16[1,15,32768]{2,1,0:T(8,128)(2,1)S(1)}, u32[]{:S(2)}, u32[]{:S(2)}) collective-permute-start(bf16[1,15,32768]{2,1,0:T(8,128)(2,1)S(1)} %get-tuple-element.9), channel_id=1, source_target_pairs={{0,1},{1,2},{2,3},{3,4},{4,5},{5,6},{6,7},{7,8},{8,9},{9,10},{10,1... | collective-permute-start | bytes 2949128 | tf_op jit(solution)/shard_map/ppermute | solution.py:19
  251.9 36.5 %collective-permute-start.3 = (bf16[1,15,32768]{2,1,0:T(8,128)(2,1)S(1)}, bf16[1,15,32768]{2,1,0:T(8,128)(2,1)S(1)}, u32[]{:S(2)}, u32[]{:S(2)}) collective-permute-start(bf16[1,15,32768]{2,1,0:T(8,128)(2,1)S(1)} %get-tuple-element.10), channel_id=1, source_target_pairs={{1,0},{2,1},{3,2},{4,3},{5,4},{6,5},{7,6},{8,7},{9,8},{10,9},{11,1... | collective-permute-start | bytes 2949128 | tf_op jit(solution)/shard_map/ppermute | solution.py:22
  290.4 3.1 %copy-start.3 = (bf16[512,512,1]{1,0,2:T(8,128)(2,1)S(1)}, bf16[512,512,1]{1,0,2:T(8,128)(2,1)}, u32[]{:S(2)}) copy-start(bf16[512,512,1]{1,0,2:T(8,128)(2,1)} %constant.50) | copy-start | bytes 1572868
  297.4 3.0 copy-start
where the time goes:
time: 302 us
  blocking collectives  136 us (45%)
  local copies, waits for them, and re-layouts  49 us (16%)
  waiting for transfers between devices  45.5 us (15%)
  other arithmetic  29.9 us (10%)
  starting transfers between devices  28.6 us (9%)
  matrix products  12.1 us (4%)
    psum x1, blocking collectives, local(): sampled = lax.psum(p_val * s_val, 'mem')  136 us
    scatter-add x1, other arithmetic, local(): adjoint = jnp.zeros((rows, LANES), jnp.float32).at[obs_row].add(contrib)  25.4 us
    ppermute x2, waiting for transfers between devices, padded_2(): lax.ppermute(lax.slice_in_dim(block, block.shape[dim] - width, None, axis...  23.5 us
    ppermute x2, waiting for transfers between devices, padded_2(): lax.ppermute(lax.slice_in_dim(block, 0, width, axis=dim), axis, backward)  22 us
    ppermute x2, starting transfers between devices, padded_2(): lax.ppermute(lax.slice_in_dim(block, 0, width, axis=dim), axis, backward)  21.9 us
    gather x1, local copies, waits for them, and re-layouts, local(): perturbations.reshape(slot_count * rows, LANES)[obs_slot * rows + obs_row]  15 us
    gather x1, local copies, waits for them, and re-layouts, local(): s_rows = smoothed.reshape(rows, LANES)[obs_row]  14.2 us
    ppermute x2, starting transfers between devices, padded_2(): lax.ppermute(lax.slice_in_dim(block, block.shape[dim] - width, None, axis...  6.69 us
  transfers between devices with their start and end apart: 4, of which 4 were waited for; matrix products, arithmetic and copies ran while one was open for 6% of the time, Pallas kernels for 0%

commit v1 on v0

--- a/solution.py
+++ b/solution.py
@@ -77,7 +77,7 @@
     s_val = jnp.sum(jnp.where(lane_hit, s_rows, 0.0), axis=1)
     p_rows = perturbations.reshape(slot_count * rows, LANES)[obs_slot * rows + obs_row]
     p_val = jnp.sum(jnp.where(lane_hit, p_rows.astype(jnp.float32), 0.0), axis=1)
-    sampled = lax.psum(p_val * s_val, "mem")
+    sampled = jnp.sum(lax.all_gather(p_val * s_val, "mem"), axis=0)
     live_mask = (jnp.arange(nobs) < obs_count[0]).astype(jnp.float32)
     residual = live_mask * obs_weight * (sampled - innovation)
     contrib = jnp.where(lane_hit, (p_val * residual)[:, None], 0.0)

time: 302 us -> 229 us (0.76)
  the two profiles are of different devices: /device:TPU:2 before, /device:TPU:1 now
where the time goes in v1:
time: 229 us
  waiting for transfers between devices  72.9 us (32%)
  blocking collectives  53.9 us (24%)
  local copies, waits for them, and re-layouts  49.1 us (21%)
  other arithmetic  29.9 us (13%)
  matrix products  12.1 us (5%)
  starting transfers between devices  9.89 us (4%)
    all_gather x1, blocking collectives, local(): sampled = jnp.sum(lax.all_gather(p_val * s_val, 'mem'), axis=0)  53.9 us
    ppermute x2, waiting for transfers between devices, padded_2(): lax.ppermute(lax.slice_in_dim(block, 0, width, axis=dim), axis, backward)  52.1 us
    scatter-add x1, other arithmetic, local(): adjoint = jnp.zeros((rows, LANES), jnp.float32).at[obs_row].add(contrib)  25.4 us
    ppermute x2, waiting for transfers between devices, padded_2(): lax.ppermute(lax.slice_in_dim(block, block.shape[dim] - width, None, axis...  20.8 us
    gather x1, local copies, waits for them, and re-layouts, local(): perturbations.reshape(slot_count * rows, LANES)[obs_slot * rows + obs_row]  15 us
    gather x1, local copies, waits for them, and re-layouts, local(): s_rows = smoothed.reshape(rows, LANES)[obs_row]  14.2 us
    ppermute x2, starting transfers between devices, padded_2(): lax.ppermute(lax.slice_in_dim(block, block.shape[dim] - width, None, axis...  7.01 us
    dot_general x2, matrix products, along_x(): jnp.einsum('ip,mpc->mic', band_x, padded, preferred_element_type=jnp.floa...  5.8 us
  transfers between devices with their start and end apart: 4, of which 3 were waited for; matrix products, arithmetic and copies ran while one was open for 8% of the time, Pallas kernels for 0%

profile of v1, /device:TPU:1, one launch (start us, length us, event | category | flops | bytes accessed | tf_op | source)
XLA Modules:
  0.0 228.6 jit_solution(9713554496768882836)
XLA Ops:
  0.0 3.1 %reshape.94 = bf16[16,512,64]{2,1,0:T(8,128)(2,1)S(1)} reshape(bf16[1,16,32768]{2,1,0:T(8,128)(2,1)} %param.13) | data formatting | bytes 2097152 | tf_op jit(solution)/shard_map/reshape
  3.1 2.4 %fusion.14 = bf16[1,16,512,64]{2,3,1,0:T(8,128)(2,1)} fusion(bf16[512,512,1]{1,0,2:T(8,128)(2,1)S(1)} %copy-done.2, bf16[64,64,1]{1,0,2:T(8,128)(2,1)S(1)} %copy-done.4, bf16[16,512,64]{2,1,0:T(8,128)(2,1)S(1)} %reshape.94), kind=kOutput, calls=%fused_computation.27 | convolution fusion | flops 605028352 | bytes 2629632 | tf_op jit(solution)/shard_map/mxqz,yq->mxyz/dot_general | solution.py:56
  5.5 2.0 copy.23
  7.6 1.7 convert_element_type.82
  9.3 1.5 fusion.25
  10.8 5.4 %collective-permute-start = (bf16[1,15,32768]{2,1,0:T(8,128)(2,1)}, bf16[1,15,32768]{2,1,0:T(8,128)(2,1)}, u32[]{:S(2)}, u32[]{:S(2)}) collective-permute-start(bf16[1,15,32768]{2,1,0:T(8,128)(2,1)} %get-tuple-element.11), channel_id=1, source_target_pairs={{0,1},{1,2},{2,3},{3,4},{4,5},{5,6},{6,7},{7,8},{8,9},{9,10},{10,1... | collective-permute-start | bytes 2949128 | tf_op jit(solution)/shard_map/ppermute | solution.py:19
  16.2 1.4 collective-permute-start.1
  17.6 2.9 %reshape.93 = bf16[8192,128]{1,0:T(8,128)(2,1)S(1)} reshape(bf16[2,1,16,32768]{3,2,1,0:T(8,128)(2,1)} %param.14) | data formatting | bytes 4194304 | tf_op jit(solution)/shard_map/reshape | solution.py:78
  21.1 0.0 copy-done.7
  21.2 0.0 copy-start.9
  21.2 15.0 %gather_fusion = bf16[4096,128]{1,0:T(8,128)(2,1)} fusion(bf16[8192,128]{1,0:T(8,128)(2,1)S(1)} %reshape.93, s32[4096]{0:T(1024)S(1)} %get-tuple-element.13), kind=kCustom, calls=%fused_computation | custom fusion | bytes 2113536 | tf_op jit(solution)/shard_map/gather | solution.py:78
  36.2 0.0 collective-permute-done
  36.2 25.7 %collective-permute-done.1 = bf16[1,15,32768]{2,1,0:T(8,128)(2,1)} collective-permute-done((bf16[1,15,32768]{2,1,0:T(8,128)(2,1)}, bf16[1,15,32768]{2,1,0:T(8,128)(2,1)}, u32[]{:S(2)}, u32[]{:S(2)}) %collective-permute-start.1) | collective-permute-done | bytes 983072 | tf_op jit(solution)/shard_map/ppermute | solution.py:22
  61.9 3.8 %convolution_bitcast_fusion = f32[1,16,32768]{2,1,0:T(8,128)} fusion(bf16[16,46]{1,0:T(8,128)(2,1)S(1)} %copy-done.9, bf16[1,15,32768]{2,1,0:T(8,128)(2,1)} %collective-permute-done.1, bf16[1,16,32768]{2,1,0:T(8,128)(2,1)S(1)} %convert_element_type.82, bf16[1,15,32768]{2,1,0:T(8,128)(2,1)} %collective-permute-done), kind=kOutput, calls=%fused_computation.3 | convolution fusion | flops 57278464 | bytes 5113280 | tf_op jit(solution)/shard_map/ip,mpc->mic/dot_general | solution.py:62
  65.8 1.7 reshape.96
  67.5 14.2 %gather_fusion.1 = f32[4096,128]{1,0:T(8,128)} fusion(f32[4096,128]{1,0:T(8,128)S(1)} %reshape.96, s32[4096]{0:T(1024)S(1)} %get-tuple-element.7), kind=kCustom, calls=%fused_computation.1 | custom fusion | bytes 4210688 | tf_op jit(solution)/shard_map/gather | solution.py:76
  81.7 2.8 %select_reduce_fusion = (f32[4096]{0:T(1024)S(1)}, f32[4096]{0:T(1024)S(1)}) fusion(f32[4096,128]{1,0:T(8,128)} %gather_fusion.1, s32[4096]{0:T(1024)S(1)} %get-tuple-element.14, bf16[4096,128]{1,0:T(8,128)(2,1)S(1)} %copy-done.1), kind=kLoop, calls=%fused_computation.16 | loop fusion | flops 3137536 | bytes 3194880 | tf_op jit(solution)/shard_map/reduce_sum | solution.py:77
  84.5 53.9 %all-gather = f32[65536]{0:T(1024)S(1)} all-gather(f32[4096]{0:T(1024)S(1)} %mul.27), channel_id=2, replica_groups=mesh['mem'=16,'gx'=32] {'mem'}, dimensions={0}, use_global_device_ids=true | all-gather | bytes 278528 | tf_op jit(solution)/shard_map/all_gather | solution.py:80
  138.4 0.1 reshape.125
  138.6 25.4 %scatter_custom_fusion = f32[4096,128]{1,0:T(8,128)S(1)} fusion(s32[4096]{0:T(1024)S(1)} %get-tuple-element.8, f32[4096]{0:T(1024)S(1)} %multiply_multiply_fusion, s32[4096]{0:T(1024)S(1)} %get-tuple-element.14, f32[]{:T(128)} %constant.34.clone.1), kind=kCustom, calls=%fused_computation.20 | custom fusion | flops 1572864 | bytes 2130944 | tf_op jit(solution)/shard_map/scatter-add | solution.py:84
  164.0 0.1 convert_element_type.83
  164.1 0.5 convert_element_type.84
  164.6 0.2 fusion.24
  164.8 1.6 collective-permute-start.2
  166.5 1.5 collective-permute-start.3
  168.0 20.8 %collective-permute-done.2 = bf16[1,15,32768]{2,1,0:T(8,128)(2,1)S(1)} collective-permute-done((bf16[1,15,32768]{2,1,0:T(8,128)(2,1)S(1)}, bf16[1,15,32768]{2,1,0:T(8,128)(2,1)S(1)}, u32[]{:S(2)}, u32[]{:S(2)}) %collective-permute-start.2) | collective-permute-done | bytes 983072 | tf_op jit(solution)/shard_map/ppermute | solution.py:19
  188.8 26.4 %collective-permute-done.3 = bf16[1,15,32768]{2,1,0:T(8,128)(2,1)S(1)} collective-permute-done((bf16[1,15,32768]{2,1,0:T(8,128)(2,1)S(1)}, bf16[1,15,32768]{2,1,0:T(8,128)(2,1)S(1)}, u32[]{:S(2)}, u32[]{:S(2)}) %collective-permute-start.3) | collective-permute-done | bytes 983072 | tf_op jit(solution)/shard_map/ppermute | solution.py:22
  215.1 2.0 fusion
  217.1 3.1 %reshape.98 = bf16[16,512,64]{2,1,0:T(8,128)(2,1)S(1)} reshape(bf16[1,16,32768]{2,1,0:T(8,128)(2,1)} %fusion) | data formatting | bytes 2097152 | tf_op jit(solution)/shard_map/reshape.9
  220.2 3.8 %fusion.15 = f32[16,512,64]{2,1,0:T(8,128)} fusion(bf16[64,64,1]{1,0,2:T(8,128)(2,1)S(1)} %copy-done.4, bf16[16,512,64]{2,1,0:T(8,128)(2,1)S(1)} %reshape.98, bf16[512,512,1]{1,0,2:T(8,128)(2,1)S(1)} %copy-done.3), kind=kOutput, calls=%fused_computation.28 | convolution fusion | flops 604504064 | bytes 3678208 | tf_op jit(solution)/shard_map/mxyq,zq->mxyz/dot_general | solution.py:48
  224.1 3.0 %reshape.100 = f32[1,16,32768]{2,1,0:T(8,128)S(1)} reshape(f32[16,512,64]{2,1,0:T(8,128)} %fusion.15) | data formatting | bytes 4194304 | tf_op jit(solution)/shard_map/reshape | solution.py:49
  227.1 1.5 convert_add_fusion
  (22 shorter events, 0.1 us)
Async XLA Ops:
  0.0 3.1 %copy-start.4 = (bf16[64,64,1]{1,0,2:T(8,128)(2,1)S(1)}, bf16[64,64,1]{1,0,2:T(8,128)(2,1)}, u32[]{:S(2)}) copy-start(bf16[64,64,1]{1,0,2:T(8,128)(2,1)} %constant.49) | copy-start | bytes 24580
  0.0 3.1 %copy-start.2 = (bf16[512,512,1]{1,0,2:T(8,128)(2,1)S(1)}, bf16[512,512,1]{1,0,2:T(8,128)(2,1)}, u32[]{:S(2)}) copy-start(bf16[512,512,1]{1,0,2:T(8,128)(2,1)} %constant.50) | copy-start | bytes 1572868
  10.8 25.4 %collective-permute-start = (bf16[1,15,32768]{2,1,0:T(8,128)(2,1)}, bf16[1,15,32768]{2,1,0:T(8,128)(2,1)}, u32[]{:S(2)}, u32[]{:S(2)}) collective-permute-start(bf16[1,15,32768]{2,1,0:T(8,128)(2,1)} %get-tuple-element.11), channel_id=1, source_target_pairs={{0,1},{1,2},{2,3},{3,4},{4,5},{5,6},{6,7},{7,8},{8,9},{9,10},{10,1... | collective-permute-start | bytes 2949128 | tf_op jit(solution)/shard_map/ppermute | solution.py:19
  16.2 5.0 %copy-start.7 = (s32[4096]{0:T(1024)S(1)}, s32[4096]{0:T(1024)}, u32[]{:S(2)}) copy-start(s32[4096]{0:T(1024)} %param.15) | copy-start | bytes 49156
  16.2 5.0 %copy-start.8 = (s32[4096]{0:T(1024)S(1)}, s32[4096]{0:T(1024)}, u32[]{:S(2)}) copy-start(s32[4096]{0:T(1024)} %param.16) | copy-start | bytes 49156
  16.2 45.8 %collective-permute-start.1 = (bf16[1,15,32768]{2,1,0:T(8,128)(2,1)}, bf16[1,15,32768]{2,1,0:T(8,128)(2,1)}, u32[]{:S(2)}, u32[]{:S(2)}) collective-permute-start(bf16[1,15,32768]{2,1,0:T(8,128)(2,1)} %get-tuple-element.12), channel_id=1, source_target_pairs={{1,0},{2,1},{3,2},{4,3},{5,4},{6,5},{7,6},{8,7},{9,8},{10,9},{11,1... | collective-permute-start | bytes 2949128 | tf_op jit(solution)/shard_map/ppermute | solution.py:22
  21.2 40.7 %copy-start.9 = (bf16[16,46]{1,0:T(8,128)(2,1)S(1)}, bf16[16,46]{1,0:T(8,128)(2,1)}, u32[]{:S(2)}) copy-start(bf16[16,46]{1,0:T(8,128)(2,1)} %constant.45.clone) | copy-start | bytes 4420
  67.5 14.2 %copy-start.1 = (bf16[4096,128]{1,0:T(8,128)(2,1)S(1)}, bf16[4096,128]{1,0:T(8,128)(2,1)}, u32[]{:S(2)}) copy-start(bf16[4096,128]{1,0:T(8,128)(2,1)} %gather_fusion) | copy-start | bytes 3145732
  81.7 56.8 %copy-start.5 = (f32[4096]{0:T(1024)S(1)}, f32[4096]{0:T(1024)}, u32[]{:S(2)}) copy-start(f32[4096]{0:T(1024)} %param.17) | copy-start | bytes 49156
  81.7 56.8 %copy-start.6 = (f32[4096]{0:T(1024)S(1)}, f32[4096]{0:T(1024)}, u32[]{:S(2)}) copy-start(f32[4096]{0:T(1024)} %param.18) | copy-start | bytes 49156
  164.8 23.9 %collective-permute-start.2 = (bf16[1,15,32768]{2,1,0:T(8,128)(2,1)S(1)}, bf16[1,15,32768]{2,1,0:T(8,128)(2,1)S(1)}, u32[]{:S(2)}, u32[]{:S(2)}) collective-permute-start(bf16[1,15,32768]{2,1,0:T(8,128)(2,1)S(1)} %get-tuple-element.9), channel_id=1, source_target_pairs={{0,1},{1,2},{2,3},{3,4},{4,5},{5,6},{6,7},{7,8},{8,9},{9,10},{10,1... | collective-permute-start | bytes 2949128 | tf_op jit(solution)/shard_map/ppermute | solution.py:19
  166.5 48.6 %collective-permute-start.3 = (bf16[1,15,32768]{2,1,0:T(8,128)(2,1)S(1)}, bf16[1,15,32768]{2,1,0:T(8,128)(2,1)S(1)}, u32[]{:S(2)}, u32[]{:S(2)}) collective-permute-start(bf16[1,15,32768]{2,1,0:T(8,128)(2,1)S(1)} %get-tuple-element.10), channel_id=1, source_target_pairs={{1,0},{2,1},{3,2},{4,3},{5,4},{6,5},{7,6},{8,7},{9,8},{10,9},{11,1... | collective-permute-start | bytes 2949128 | tf_op jit(solution)/shard_map/ppermute | solution.py:22
  217.1 3.1 %copy-start.3 = (bf16[512,512,1]{1,0,2:T(8,128)(2,1)S(1)}, bf16[512,512,1]{1,0,2:T(8,128)(2,1)}, u32[]{:S(2)}) copy-start(bf16[512,512,1]{1,0,2:T(8,128)(2,1)} %constant.50) | copy-start | bytes 1572868
  224.1 3.0 %copy-start = (bf16[1,16,32768]{2,1,0:T(8,128)(2,1)S(1)}, bf16[1,16,32768]{2,1,0:T(8,128)(2,1)}, u32[]{:S(2)}) copy-start(bf16[1,16,32768]{2,1,0:T(8,128)(2,1)} %param.13) | copy-start | bytes 3145732
